TPU v7x, 256 devices: a whole 4x4x8 slice. The times are simulated.
256 devices in a mesh: req: 32 (over x, y, core), kv: 8 (over z).
Axes of the slice: x: 4, y: 4, z: 8, core: 2. Of those that a mesh axis runs over, the one named last changes fastest.
Arguments:
- hidden: bfloat16 [512, 1536], P('req'), may hold values from -6 to 6
- norm_gain: float32 [1536], replicated, may hold values from 0.5 to 1.5
- w_qkv: bfloat16 [1536, 3072], P(None, 'kv'), may hold values from -0.15625 to 0.15625
- w_out: bfloat16 [1536, 1536], P(None, 'kv'), may hold values from -0.15625 to 0.15625
- cache_pages: bfloat16 [6144, 2, 8, 96, 128], P('req', None, 'kv'), may hold values from -340 to 340
- lengths: int32 [512], P('req'), may hold values from 1 to 16384, as said below
- page_table: int32 [512, 128], P('req'), may hold values from 0 to 191, as said below
- occupant: int32 [512], replicated, may hold values from 0 to 511, each once
Outputs:
- mixed: bfloat16 [512, 1536], P('req', 'kv')
Inputs may be any that keep to these rules, and one draw needn't show every extreme that they name: `occupant`: every request is served at exactly one slot. Slot s holds ceil(lengths[s] / 128) pages; on every index of req the pages of its 16 slots fit its pool of 192, some pool is full, and some request has 16384 tokens. `page_table`: the first ceil(lengths[s] / 128) entries of slot s are pages of its own pool that no other slot of that pool uses; later entries are arbitrary pages of the pool.
All inputs are finite; a program needn't handle non-finite values.
Results may differ from a plain program's by a relative error of at most 0.0043.
Values may be sent and summed in bfloat16 or wider, within the bound.
No kernel may reach another device: no remote copies, remote signals or barrier semaphores. Data moves between devices by JAX's collectives and lax.ppermute only.
A program may use at most 64 MiB of HBM per device.

v0:
```python
import math
import jax
import jax.numpy as jnp
from jax import lax
from jax.sharding import PartitionSpec as P

HD = 96
PAGE = 128
MAXP = 128
GROUP = 2


def per_device(hidden, norm_gain, w_qkv, w_out, cache_pages, lengths, page_table, occupant):
    slot_count = hidden.shape[0]
    pool_size = cache_pages.shape[0]
    kv_local = cache_pages.shape[2]
    first_slot = lax.axis_index("req") * slot_count
    hidden_wide = hidden.astype(jnp.float32)
    normed = (
        hidden_wide
        * lax.rsqrt(jnp.mean(hidden_wide * hidden_wide, axis=1, keepdims=True) + 1e-05)
        * norm_gain
    ).astype(jnp.bfloat16)
    served = lax.dynamic_slice_in_dim(occupant, first_slot, slot_count)
    own_rows = jnp.dot(normed, w_qkv, preferred_element_type=jnp.float32).astype(jnp.bfloat16)
    every_row = lax.all_gather(own_rows, "req", axis=0, tiled=True)
    slot_rows = jnp.take(every_row, served, axis=0)
    slot_rows = slot_rows.reshape(slot_count, kv_local, GROUP + 2, HD)
    queries = slot_rows[:, :, :GROUP]
    own_key = slot_rows[:, :, GROUP]
    own_value = slot_rows[:, :, GROUP + 1]
    score_scale = 1.0 / math.sqrt(HD)
    pages_used = (lengths + PAGE - 1) // PAGE
    live_page = jnp.arange(MAXP, dtype=jnp.int32)[None, :] < pages_used[:, None]
    matches = (
        (page_table[:, :, None] == jnp.arange(pool_size, dtype=jnp.int32)[None, None, :])
        & live_page[:, :, None]
    ).astype(jnp.int32)
    owner_table = jnp.sum(matches, axis=1)
    slot_ids = jnp.arange(slot_count, dtype=jnp.int32)
    page_owner = jnp.sum(owner_table * slot_ids[:, None], axis=0)
    page_rank = jnp.sum(matches * jnp.arange(MAXP, dtype=jnp.int32)[None, :, None], axis=(0, 1))
    page_limit = jnp.sum(owner_table * lengths[:, None], axis=0)
    offsets = page_rank[:, None] * PAGE + jnp.arange(PAGE, dtype=jnp.int32)[None, :]
    token_live = offsets < page_limit[:, None]
    page_queries = jnp.take(queries, page_owner, axis=0)
    scores = (
        jnp.einsum(
            "pgjd,pgdt->pgjt", page_queries, cache_pages[:, 0], preferred_element_type=jnp.float32
        )
        * score_scale
    )
    scores = jnp.where(token_live[:, None, None, :], scores, -jnp.inf)
    page_max = jnp.max(scores, axis=-1)
    own_score = (
        jnp.sum(queries.astype(jnp.float32) * own_key.astype(jnp.float32)[:, :, None, :], axis=-1)
        * score_scale
    )
    owner_mask = owner_table > 0
    slot_max = jnp.max(jnp.where(owner_mask[:, :, None, None], page_max[None], -jnp.inf), axis=1)
    slot_max = jnp.maximum(slot_max, own_score)
    weights = jnp.exp(scores - jnp.take(slot_max, page_owner, axis=0)[..., None])
    rounded = weights.astype(jnp.bfloat16)
    page_total = jnp.sum(weights, axis=-1)
    page_numerator = jnp.einsum(
        "pgjt,pgdt->pgjd", rounded, cache_pages[:, 1], preferred_element_type=jnp.float32
    )
    own_weight = jnp.exp(own_score - slot_max)
    own_rounded = lax.optimization_barrier(own_weight.astype(jnp.bfloat16)).astype(jnp.float32)
    owner_float = owner_table.astype(jnp.float32)
    denominator = (
        jnp.einsum("sp,pgj->sgj", owner_float, page_total, precision=lax.Precision.HIGHEST)
        + own_weight
    )
    numerator = jnp.einsum(
        "sp,pgjd->sgjd", owner_float, page_numerator, precision=lax.Precision.HIGHEST
    )
    numerator = numerator + own_rounded[..., None] * own_value.astype(jnp.float32)[:, :, None, :]
    context = (numerator / denominator[..., None]).astype(jnp.bfloat16).reshape(slot_count, -1)
    gathered = lax.all_gather(context, "req", axis=0, tiled=True)
    wanted = first_slot + slot_ids
    selector = (occupant[None, :] == wanted[:, None]).astype(jnp.bfloat16)
    attended = jnp.dot(selector, gathered, preferred_element_type=jnp.float32).astype(jnp.bfloat16)
    partial_value = lax.dot_general(
        attended, w_out, (((1,), (1,)), ((), ())), preferred_element_type=jnp.float32
    )
    summed = lax.psum_scatter(partial_value, "kv", scatter_dimension=1, tiled=True)
    col_share = summed.shape[1]
    residual = lax.dynamic_slice_in_dim(hidden_wide, lax.axis_index("kv") * col_share, col_share, 1)
    return (residual + summed).astype(jnp.bfloat16)


def solution(mesh):
    return jax.shard_map(
        per_device,
        mesh=mesh,
        in_specs=(
            P("req", None),
            P(),
            P(None, "kv"),
            P(None, "kv"),
            P("req", None, "kv", None, None),
            P("req"),
            P("req", None),
            P(),
        ),
        out_specs=P("req", "kv"),
        check_vma=False,
    )
```

profile of v0, /device:TPU:2, one launch (start us, length us, event | category | flops | bytes accessed | tf_op | source)
XLA Modules:
  0.0 121.7 jit_solution(13815415741669483195)
XLA Ops:
  6.6 0.9 compare_and_fusion
  7.4 0.9 multiply_reduce_fusion
  8.4 1.1 convolution_convert_fusion
  9.5 24.9 %all_gather.6 = bf16[512,384]{1,0:T(8,128)(2,1)S(1)} all-gather(bf16[16,384]{1,0:T(8,128)(2,1)S(1)} %convolution_convert_fusion), channel_id=1, replica_groups=mesh['req'=32,'kv'=8] {'req'}, dimensions={0}, use_global_device_ids=true | all-gather | bytes 405504 | tf_op jit(solution)/shard_map/all_gather | solution.py:26
  34.4 0.6 gather_fusion
  35.0 0.1 gather.19
  35.1 0.1 broadcast_select_fusion.3
  35.2 0.1 iota_compare_fusion.1
  35.3 1.0 select_reduce_fusion
  36.3 0.1 multiply_reduce_fusion.2
  36.4 0.1 multiply_reduce_fusion.1
  36.5 0.1 copy.29
  36.6 0.8 gather_fusion.1
  37.5 0.1 add_compare_fusion
  37.6 3.8 %fusion.38 = (f32[192,2]{1,0:T(8,128)S(1)}, f32[192,2,128]{2,1,0:T(2,128)S(1)}) fusion(bf16[192,2,1,96,128]{4,3,2,1,0:T(8,128)(2,1)} %param.12, bf16[192,2,96]{2,1,0:T(2,128)(2,1)S(1)} %gather_fusion.1, pred[192]{0:T(512)(128)(4,1)S(1)} %compare_and_fusion.1, pred[192,128]{1,0:T(8,128)(4,1)S(1)} %add_compare_fusion), kind=kOutput, calls=%fused_computation.76 | convolution fusion | flops 9621120 | bytes 5015232 | tf_op jit(solution)/shard_map/pgjd,pgdt->pgjt/dot_general | solution.py:48
  41.4 0.1 copy.28
  41.5 0.1 select_reduce_fusion.1
  41.6 0.1 copy.30
  41.7 0.7 gather_fusion.2
  42.4 0.1 broadcast_select_fusion.2
  42.5 0.5 fusion.16
  43.1 0.0 copy-start.1
  43.1 5.0 %fusion = f32[192,2,96]{2,1,0:T(2,128)S(1)} fusion(bf16[192,2,1,96,128]{4,3,2,1,0:T(8,128)(2,1)} %param.12, f32[192,2,128]{2,1,0:T(2,128)S(1)} %get-tuple-element.16, f32[192,2]{1,0:T(8,128)S(1)} %broadcast_select_fusion.2), kind=kOutput, calls=%fused_computation.3 | convolution fusion | flops 9535488 | bytes 5064192 | tf_op jit(solution)/shard_map/pgjt,pgdt->pgjd/dot_general | solution.py:65
  48.1 0.3 convolution_add_fusion.1
  48.4 0.3 fusion.11
  48.7 0.1 reshape.245
  48.7 23.1 %all_gather.7 = bf16[512,192]{1,0:T(8,128)(2,1)S(1)} all-gather(bf16[16,192]{1,0:T(8,128)(2,1)S(1)} %reshape.245), channel_id=1, replica_groups=mesh['req'=32,'kv'=8] {'req'}, dimensions={0}, use_global_device_ids=true | all-gather | bytes 202752 | tf_op jit(solution)/shard_map/all_gather | solution.py:80
  71.8 1.5 %convolution_bitcast_fusion = f32[1536,16]{1,0:T(8,128)} fusion(bf16[1536,192]{0,1:T(8,128)(2,1)S(1)} %copy-done.1, bf16[512,192]{1,0:T(8,128)(2,1)S(1)} %all_gather.7, s32[512]{0:T(512)S(1)} %copy-done.4, s32[16]{0:T(128)S(1)} %iota_add_fusion), kind=kOutput, calls=%fused_computation.9 | convolution fusion | flops 12594176 | bytes 886848
  73.3 0.0 reduce-scatter.4.cloned.1.call-update
  73.3 39.9 %reduce-scatter.4.cloned.1.call-done = f32[192,16]{1,0:T(8,128)} async-done(((f32[1536,16]{1,0:T(8,128)}), f32[192,16]{1,0:T(8,128)}) %reduce-scatter.4.cloned.1.call-update) | async-done | bytes 12304
  113.2 0.9 copy.35
  114.2 0.7 add_convert_fusion
  (27 shorter events, 0.1 us)
Async XLA Ops:
  6.5 1.8 %copy-start = (bf16[1536,384]{1,0:T(8,128)(2,1)S(1)}, bf16[1536,384]{1,0:T(8,128)(2,1)}, u32[]{:S(2)}) copy-start(bf16[1536,384]{1,0:T(8,128)(2,1)} %param.10) | copy-start | bytes 3538948
  6.5 28.7 %copy-start.5 = (s32[16]{0:T(128)S(1)}, s32[16]{0:T(128)}, u32[]{:S(2)}) copy-start(s32[16]{0:T(128)} %param.13) | copy-start | bytes 196
  6.5 28.8 %copy-start.3 = (s32[16,128]{1,0:T(8,128)S(1)}, s32[16,128]{1,0:T(8,128)}, u32[]{:S(2)}) copy-start(s32[16,128]{1,0:T(8,128)} %param.14) | copy-start | bytes 24580
  6.5 106.7 %reduce-scatter.4.cloned.1.call-start = ((), (), s32[]{:S(2)}) async-start(), calls=%async_computation.1 | async-start | bytes 884736
  43.1 28.8 %copy-start.1 = (bf16[1536,192]{0,1:T(8,128)(2,1)S(1)}, bf16[1536,192]{0,1:T(8,128)(2,1)}, u32[]{:S(2)}) copy-start(bf16[1536,192]{0,1:T(8,128)(2,1)} %param.11) | copy-start | bytes 1769476
  43.1 28.7 %copy-start.4 = (s32[512]{0:T(512)S(1)}, s32[512]{0:T(512)}, u32[]{:S(2)}) copy-start(s32[512]{0:T(512)} %param.15) | copy-start | bytes 6148
  48.1 25.2 %copy-start.2 = (bf16[16,1536]{1,0:T(8,128)(2,1)S(1)}, bf16[16,1536]{1,0:T(8,128)(2,1)}, u32[]{:S(2)}) copy-start(bf16[16,1536]{1,0:T(8,128)(2,1)} %param.8) | copy-start | bytes 147460
Sparse Core Ops, SparseCore 0:
  73.4 39.7 reduce-scatter.3
where the time goes:
time: 122 us
  blocking collectives  47.9 us (39%)
  waiting for transfers between devices  39.9 us (33%)
  between operations  13.6 us (11%)
  matrix products  12 us (10%)
  other arithmetic  4.73 us (4%)
  local copies, waits for them, and re-layouts  3.55 us (3%)
    unnamed x2, waiting for transfers between devices  39.9 us
    all_gather x1, blocking collectives, per_device(): every_row = lax.all_gather(own_rows, 'req', axis=0, tiled=True)  24.9 us
    all_gather x1, blocking collectives, per_device(): gathered = lax.all_gather(context, 'req', axis=0, tiled=True)  23.1 us
    dot_general x1, matrix products, per_device(): jnp.einsum('pgjt,pgdt->pgjd', rounded, cache_pages[:, 1], preferred_eleme...  5.01 us
    dot_general x1, matrix products, per_device(): jnp.einsum('pgjd,pgdt->pgjt', page_queries, cache_pages[:, 0], preferred_...  3.85 us
  transfers between devices with their start and end apart: 1, of which 1 were waited for; matrix products, arithmetic and copies ran while one was open for 0% of the time, Pallas kernels for 0%

commit v1 on v0

--- a/solution.py
+++ b/solution.py
@@ -77,7 +77,9 @@
     )
     numerator = numerator + own_rounded[..., None] * own_value.astype(jnp.float32)[:, :, None, :]
     context = (numerator / denominator[..., None]).astype(jnp.bfloat16).reshape(slot_count, -1)
-    gathered = lax.all_gather(context, "req", axis=0, tiled=True)
+    gathered = jnp.concatenate(
+        lax.all_to_all(jnp.stack([context] * lax.axis_size("req")), "req", 0, 0), axis=0
+    )
     wanted = first_slot + slot_ids
     selector = (occupant[None, :] == wanted[:, None]).astype(jnp.bfloat16)
     attended = jnp.dot(selector, gathered, preferred_element_type=jnp.float32).astype(jnp.bfloat16)

time: 122 us -> 112 us (0.918)
  blocking collectives: 47.9 us -> 24.9 us
  waiting for transfers between devices: 39.9 us -> 46.3 us
  starting transfers between devices: 0.01 us -> 5.76 us
    all_gather x1 -> x0, blocking collectives: 23.1 us -> none  [per_device(): gathered = lax.all_gather(context, 'req', axis=0, tiled=True)]
    all_to_all x0 -> x1, waiting for transfers between devices: none -> 7.63 us  [per_device(): lax.all_to_all(jnp.stack([context] * lax.axis_size('req')), 'req', 0, 0)]
    all_to_all x0 -> x1, starting transfers between devices: none -> 5.72 us  [per_device(): lax.all_to_all(jnp.stack([context] * lax.axis_size('req')), 'req', 0, 0)]
  transfers between devices with their start and end apart: 1 -> 2, of which waited for: 1 -> 2; matrix products, arithmetic and copies ran while one was open for 0% -> 0% of each run, Pallas kernels for 0% -> 0%
where the time goes in v1:
time: 112 us
  waiting for transfers between devices  46.3 us (41%)
  blocking collectives  24.9 us (22%)
  between operations  13.6 us (12%)
  matrix products  12 us (11%)
  starting transfers between devices  5.76 us (5%)
  other arithmetic  4.73 us (4%)
  local copies, waits for them, and re-layouts  4.25 us (4%)
    unnamed x2, waiting for transfers between devices  38.7 us
    all_gather x1, blocking collectives, per_device(): every_row = lax.all_gather(own_rows, 'req', axis=0, tiled=True)  24.9 us
    all_to_all x1, waiting for transfers between devices, per_device(): lax.all_to_all(jnp.stack([context] * lax.axis_size('req')), 'req', 0, 0)  7.63 us
    all_to_all x1, starting transfers between devices, per_device(): lax.all_to_all(jnp.stack([context] * lax.axis_size('req')), 'req', 0, 0)  5.72 us
    dot_general x1, matrix products, per_device(): jnp.einsum('pgjt,pgdt->pgjd', rounded, cache_pages[:, 1], preferred_eleme...  4.95 us
    dot_general x1, matrix products, per_device(): jnp.einsum('pgjd,pgdt->pgjt', page_queries, cache_pages[:, 0], preferred_...  3.85 us
  transfers between devices with their start and end apart: 2, of which 2 were waited for; matrix products, arithmetic and copies ran while one was open for 0% of the time, Pallas kernels for 0%

profile of v1, /device:TPU:2, one launch (start us, length us, event | category | flops | bytes accessed | tf_op | source)
XLA Modules:
  0.0 111.5 jit_solution(7787076767201274260)
XLA Ops:
  6.5 0.9 compare_and_fusion
  7.4 0.9 multiply_reduce_fusion
  8.3 1.1 %convolution_convert_fusion = bf16[16,384]{1,0:T(8,128)(2,1)S(1)} fusion(bf16[1536,384]{1,0:T(8,128)(2,1)S(1)} %copy-done, f32[1536]{0:T(1024)} %param.9, f32[16]{0:T(128)S(1)} %add_rsqrt_fusion, bf16[16,1536]{1,0:T(8,128)(2,1)} %param.8), kind=kOutput, calls=%fused_computation.15 | convolution fusion | flops 18978816 | bytes 1247296 | tf_op jit(solution)/shard_map/dot_general | solution.py:25
  9.5 24.9 %all_gather.3 = bf16[512,384]{1,0:T(8,128)(2,1)S(1)} all-gather(bf16[16,384]{1,0:T(8,128)(2,1)S(1)} %convolution_convert_fusion), channel_id=1, replica_groups=mesh['req'=32,'kv'=8] {'req'}, dimensions={0}, use_global_device_ids=true | all-gather | bytes 405504 | tf_op jit(solution)/shard_map/all_gather | solution.py:26
  34.4 0.6 gather_fusion
  35.0 0.1 gather.19
  35.0 0.1 broadcast_select_fusion.3
  35.2 0.1 iota_compare_fusion.1
  35.3 1.0 select_reduce_fusion
  36.3 0.1 multiply_reduce_fusion.2
  36.4 0.1 multiply_reduce_fusion.1
  36.5 0.1 copy.29
  36.6 0.8 gather_fusion.1
  37.4 0.1 add_compare_fusion
  37.6 3.9 %fusion.38 = (f32[192,2]{1,0:T(8,128)S(1)}, f32[192,2,128]{2,1,0:T(2,128)S(1)}) fusion(bf16[192,2,1,96,128]{4,3,2,1,0:T(8,128)(2,1)} %param.12, bf16[192,2,96]{2,1,0:T(2,128)(2,1)S(1)} %gather_fusion.1, pred[192]{0:T(512)(128)(4,1)S(1)} %compare_and_fusion.1, pred[192,128]{1,0:T(8,128)(4,1)S(1)} %add_compare_fusion), kind=kOutput, calls=%fused_computation.76 | convolution fusion | flops 9621120 | bytes 5015232 | tf_op jit(solution)/shard_map/pgjd,pgdt->pgjt/dot_general | solution.py:48
  41.4 0.1 copy.28
  41.5 0.1 select_reduce_fusion.1
  41.6 0.1 copy.30
  41.7 0.7 gather_fusion.2
  42.4 0.1 broadcast_select_fusion.2
  42.5 0.5 fusion.16
  43.1 5.0 %fusion = f32[192,2,96]{2,1,0:T(2,128)S(1)} fusion(bf16[192,2,1,96,128]{4,3,2,1,0:T(8,128)(2,1)} %param.12, f32[192,2,128]{2,1,0:T(2,128)S(1)} %get-tuple-element.16, f32[192,2]{1,0:T(8,128)S(1)} %broadcast_select_fusion.2), kind=kOutput, calls=%fused_computation.3 | convolution fusion | flops 9535488 | bytes 5064192 | tf_op jit(solution)/shard_map/pgjt,pgdt->pgjd/dot_general | solution.py:65
  48.0 0.3 convolution_add_fusion.1
  48.3 0.3 fusion.11
  48.6 0.1 stack_reshape.2
  48.7 0.7 stack.3
  49.4 5.7 %all-to-all-start = ((bf16[32,16,192]{2,1,0:T(8,128)(2,1)}), bf16[32,16,192]{2,1,0:T(8,128)(2,1)S(1)}, u32[]{:S(2)}, u32[]{:S(2)}) async-start(bf16[32,16,192]{2,1,0:T(8,128)(2,1)} %stack.3), calls=%async_computation | async-start | bytes 524288 | tf_op jit(solution)/shard_map/all_to_all | solution.py:81
  55.2 7.6 %all-to-all-done = bf16[32,16,192]{2,1,0:T(8,128)(2,1)S(1)} async-done(((bf16[32,16,192]{2,1,0:T(8,128)(2,1)}), bf16[32,16,192]{2,1,0:T(8,128)(2,1)S(1)}, u32[]{:S(2)}, u32[]{:S(2)}) %all-to-all-start) | async-done | bytes 196640 | tf_op jit(solution)/shard_map/all_to_all | solution.py:81
  62.8 1.5 %convolution_bitcast_fusion = f32[1536,16]{1,0:T(8,128)} fusion(bf16[1536,192]{0,1:T(8,128)(2,1)S(1)} %copy-done.1, bf16[512,192]{1,0:T(8,128)(2,1)S(1)} %bitcast.55, s32[512]{0:T(512)S(1)} %copy-done.4, s32[16]{0:T(128)S(1)} %iota_add_fusion), kind=kOutput, calls=%fused_computation.9 | convolution fusion | flops 12594176 | bytes 886848
  64.4 38.7 %reduce-scatter.4.cloned.1.call-done = f32[192,16]{1,0:T(8,128)} async-done(((f32[1536,16]{1,0:T(8,128)}), f32[192,16]{1,0:T(8,128)}) %reduce-scatter.4.cloned.1.call-update) | async-done | bytes 12304
  103.0 0.9 copy.35
  104.0 0.7 add_convert_fusion
  (29 shorter events, 0.2 us)
Async XLA Ops:
  6.5 1.8 %copy-start = (bf16[1536,384]{1,0:T(8,128)(2,1)S(1)}, bf16[1536,384]{1,0:T(8,128)(2,1)}, u32[]{:S(2)}) copy-start(bf16[1536,384]{1,0:T(8,128)(2,1)} %param.10) | copy-start | bytes 3538948
  6.5 28.6 %copy-start.5 = (s32[16]{0:T(128)S(1)}, s32[16]{0:T(128)}, u32[]{:S(2)}) copy-start(s32[16]{0:T(128)} %param.13) | copy-start | bytes 196
  6.5 28.7 %copy-start.3 = (s32[16,128]{1,0:T(8,128)S(1)}, s32[16,128]{1,0:T(8,128)}, u32[]{:S(2)}) copy-start(s32[16,128]{1,0:T(8,128)} %param.14) | copy-start | bytes 24580
  43.0 19.8 %copy-start.4 = (s32[512]{0:T(512)S(1)}, s32[512]{0:T(512)}, u32[]{:S(2)}) copy-start(s32[512]{0:T(512)} %param.15) | copy-start | bytes 6148
  48.0 14.8 %copy-start.1 = (bf16[1536,192]{0,1:T(8,128)(2,1)S(1)}, bf16[1536,192]{0,1:T(8,128)(2,1)}, u32[]{:S(2)}) copy-start(bf16[1536,192]{0,1:T(8,128)(2,1)} %param.11) | copy-start | bytes 1769476
  48.7 15.7 %copy-start.2 = (bf16[16,1536]{1,0:T(8,128)(2,1)S(1)}, bf16[16,1536]{1,0:T(8,128)(2,1)}, u32[]{:S(2)}) copy-start(bf16[16,1536]{1,0:T(8,128)(2,1)} %param.8) | copy-start | bytes 147460
  49.4 13.4 %all-to-all-start = ((bf16[32,16,192]{2,1,0:T(8,128)(2,1)}), bf16[32,16,192]{2,1,0:T(8,128)(2,1)S(1)}, u32[]{:S(2)}, u32[]{:S(2)}) async-start(bf16[32,16,192]{2,1,0:T(8,128)(2,1)} %stack.3), calls=%async_computation | async-start | bytes 524288 | tf_op jit(solution)/shard_map/all_to_all | solution.py:81
  55.1 47.9 %reduce-scatter.4.cloned.1.call-start = ((), (), s32[]{:S(2)}) async-start(), calls=%async_computation.2 | async-start | bytes 884736
Sparse Core Ops, SparseCore 0:
  64.4 38.5 reduce-scatter.3
